TPU v7x, 256 devices: a whole 4x4x8 slice. The times are simulated.
256 devices in a mesh: tok: 64 (over y, z, core), head: 4 (over x).
Axes of the slice: x: 4, y: 4, z: 8, core: 2. Of those that a mesh axis runs over, the one named last changes fastest.
Arguments:
- hidden: bfloat16 [2048, 2048], P('tok', 'head'), may hold values from -24 to 24
- attn_gain: float32 [2048], replicated, may hold values from 0.1 to 1.9
- w_query: bfloat16 [2048, 3072], P(None, 'head'), may hold values from -0.125 to 0.125
- w_latent: bfloat16 [2048, 576], P('head'), may hold values from -0.125 to 0.125
- w_key_up: bfloat16 [16, 128, 512], P('head'), may hold values from -0.5 to 0.5
- w_value_up: bfloat16 [16, 512, 128], P('head'), may hold values from -1 to 1
- w_out: bfloat16 [2048, 2048], P('head'), may hold values from -0.125 to 0.125
- latent_cache: bfloat16 [638976, 576], P(('tok', 'head')), may hold values from -6 to 6
- cache_lengths: int32 [2048], P('tok'), may hold values from 144 to 2048, as said below
- request_slot: int32 [2048], P('tok'), may hold values from 0 to 2047, as said below
- ffn_gain: float32 [2048], P('head'), may hold values from 0.1 to 1.9
- w_router: bfloat16 [2048, 64], P('head'), may hold values from -0.25 to 0.25
- routes: int32 [2048, 6], P('tok'), may hold values from 0 to 63, all different within a row; in each aligned block of 32 rows (0 to 31, 32 to 63, ...) at most 6 rows name the same one
- expert_gate: bfloat16 [64, 2048, 1408], P('tok', None, 'head'), may hold values from -0.125 to 0.125
- expert_up: bfloat16 [64, 2048, 1408], P('tok', None, 'head'), may hold values from -0.125 to 0.125
- expert_down: bfloat16 [64, 1408, 2048], P('tok', 'head'), may hold values from -0.15625 to 0.15625
Outputs:
- new_entry: bfloat16 [2048, 576], P('tok')
- attended: bfloat16 [2048, 2048], P('tok', 'head')
- expert_mix: bfloat16 [2048, 2048], P('tok', 'head')
Inputs may be any that keep to these rules, and one draw needn't show every extreme that they name: `request_slot`: a permutation of the 2048 slots; slot s lies on owner s // 32, so every owner holds 32 slots; the requests of one device name at most 1 slots of one owner, and every device reaches that bound. `cache_lengths`: the caches of an owner's slots lie end to end in slot order at the start of that owner's 9984 rows of latent_cache; they fill at most 9984 rows, and some owner fills all of them. `routes`: each row names 6 different experts; in the rows of one device no expert is named more than 6 times.
All inputs are finite; a program needn't handle non-finite values.
Results may differ from a plain program's by a relative error of at most 0.028.
Values may be sent and summed in bfloat16 or wider, within the bound.
No kernel may reach another device: no remote copies, remote signals or barrier semaphores. Data moves between devices by JAX's collectives and lax.ppermute only.
A program may use at most 128 MiB of HBM per device.

v0:
```python
import jax
import jax.numpy as jnp
from jax import lax
from jax.sharding import PartitionSpec as P

D = 2048
NOPE = 128
ROPE = 64
LATENT = 512
NORM_EPS = 1e-06


def rotate_pairs(values, places):
    halfway = values.shape[-1] // 2
    freqs = 10000.0 ** (-jnp.arange(halfway, dtype=jnp.float32) / halfway)
    angles = places.astype(jnp.float32).reshape(places.shape + (1,) * (values.ndim - 1)) * freqs
    cosine = jnp.cos(angles)
    sine = jnp.sin(angles)
    first_half = values[..., :halfway]
    second_half = values[..., halfway:]
    return jnp.concatenate(
        [first_half * cosine - second_half * sine, first_half * sine + second_half * cosine],
        axis=-1,
    )


def owner_attend(all_heads, owner_lengths, latent_cache, head_index, factor):
    slot_rows = all_heads.shape[0]
    total_heads = all_heads.shape[1]
    probe_width = all_heads.shape[2]
    key_rows = latent_cache.shape[0]
    starts = jnp.cumsum(owner_lengths) - owner_lengths
    places = head_index * key_rows + jnp.arange(key_rows, dtype=jnp.int32)
    inside = (places[None, :] >= starts[:, None]) & (
        places[None, :] < (starts + owner_lengths)[:, None]
    )
    scores = factor * jnp.einsum(
        "qc,pc->qp",
        all_heads.reshape(slot_rows * total_heads, probe_width),
        latent_cache,
        preferred_element_type=jnp.float32,
    )
    scores = scores.reshape(slot_rows, total_heads, key_rows)
    weights = jnp.where(inside[:, None, :], jnp.exp(scores), 0.0).astype(jnp.bfloat16)
    numerator = jnp.einsum(
        "khp,pl->khl", weights, latent_cache[:, :LATENT], preferred_element_type=jnp.float32
    )
    denominator = jnp.sum(weights.astype(jnp.float32), axis=2)
    return (numerator, denominator)


def body(
    hidden,
    attn_gain,
    w_query,
    w_latent,
    w_key_up,
    w_value_up,
    w_out,
    latent_cache,
    cache_lengths,
    request_slot,
    ffn_gain,
    w_router,
    routes,
    expert_gate,
    expert_up,
    expert_down,
):
    local_rows = hidden.shape[0]
    quarter_width = hidden.shape[1]
    local_heads = w_key_up.shape[0]
    peer_count = lax.axis_size("tok")
    head_index = lax.axis_index("head")
    tok_index = lax.axis_index("tok")
    row_ids = jnp.arange(local_rows, dtype=jnp.int32)
    gathered = lax.all_gather(hidden, "head", axis=1, tiled=True)
    widened = gathered.astype(jnp.float32)
    inv_attn = lax.rsqrt(jnp.mean(widened * widened, axis=1, keepdims=True) + NORM_EPS)
    normed_attn = (widened * inv_attn * attn_gain).astype(jnp.bfloat16)
    normed_part = lax.dynamic_slice_in_dim(
        normed_attn, head_index * quarter_width, quarter_width, 1
    )
    compressed = lax.psum(
        jnp.dot(normed_part, w_latent, preferred_element_type=jnp.float32), "head"
    )
    latent_new = compressed[:, :LATENT]
    latent_new = latent_new * lax.rsqrt(
        jnp.mean(latent_new * latent_new, axis=1, keepdims=True) + NORM_EPS
    )
    new_entry = jnp.concatenate(
        [latent_new, rotate_pairs(compressed[:, LATENT:], cache_lengths)], axis=1
    ).astype(jnp.bfloat16)
    queries = jnp.dot(normed_attn, w_query, preferred_element_type=jnp.float32).astype(jnp.bfloat16)
    queries = queries.reshape(local_rows, local_heads, NOPE + ROPE)
    absorbed = jnp.einsum(
        "bhn,hnl->bhl", queries[:, :, :NOPE], w_key_up, preferred_element_type=jnp.float32
    ).astype(jnp.bfloat16)
    turned = rotate_pairs(queries[:, :, NOPE:].astype(jnp.float32), cache_lengths).astype(
        jnp.bfloat16
    )
    probes = jnp.concatenate([absorbed, turned], axis=2)
    factor = (NOPE + ROPE) ** (-0.5)
    self_score = factor * jnp.einsum(
        "bhc,bc->bh", probes, new_entry, preferred_element_type=jnp.float32
    )
    self_weight = jnp.exp(self_score).astype(jnp.bfloat16).astype(jnp.float32)
    per_owner = max(1, local_rows // peer_count)
    buffer_rows = peer_count * per_owner
    buffer_ids = jnp.arange(buffer_rows, dtype=jnp.int32)
    dest_owner = request_slot // local_rows
    earlier_same = (dest_owner[None, :] == dest_owner[:, None]) & (
        row_ids[None, :] < row_ids[:, None]
    )
    send_place = dest_owner * per_owner + jnp.sum(earlier_same.astype(jnp.int32), axis=1)
    all_probes, all_slots, all_lengths = (
        lax.all_gather(probes, "tok", axis=0, tiled=True),
        lax.all_gather(request_slot, "tok", axis=0, tiled=True),
        lax.all_gather(cache_lengths, "tok", axis=0, tiled=True),
    )
    total_rows = all_slots.shape[0]
    slot_hit = all_slots[None, :] == (tok_index * local_rows + row_ids)[:, None]
    request_at = jnp.sum(
        jnp.where(slot_hit, jnp.arange(total_rows, dtype=jnp.int32)[None, :], 0), axis=1
    )
    owner_probes = all_probes[request_at]
    owner_lengths = all_lengths[request_at]
    owned_here = (
        (all_slots // local_rows == tok_index).astype(jnp.int32).reshape(peer_count, local_rows)
    )
    prior_count = (jnp.cumsum(owned_here, axis=1) - owned_here).reshape(total_rows)
    back_index = request_at // local_rows * per_owner + prior_count[request_at]
    all_heads = lax.all_gather(owner_probes, "head", axis=1, tiled=True)
    numerator, denominator = owner_attend(
        all_heads, owner_lengths, latent_cache, head_index, factor
    )
    group_num, group_den = (
        lax.psum_scatter(numerator, "head", scatter_dimension=1, tiled=True),
        lax.psum_scatter(denominator, "head", scatter_dimension=1, tiled=True),
    )
    at_place = buffer_ids[:, None] == back_index[None, :]
    slot_of_place = jnp.sum(jnp.where(at_place, row_ids[None, :], 0), axis=1) + local_rows * (
        1 - jnp.max(at_place.astype(jnp.int32), axis=1)
    )
    padded_num = jnp.concatenate(
        [group_num, jnp.zeros((1, local_heads, LATENT), jnp.float32)], axis=0
    )
    padded_den = jnp.concatenate([group_den, jnp.zeros((1, local_heads), jnp.float32)], axis=0)
    got_num, got_den = (
        lax.all_to_all(
            padded_num[slot_of_place].reshape(peer_count, per_owner, local_heads, LATENT),
            "tok",
            split_axis=0,
            concat_axis=0,
            tiled=True,
        ),
        lax.all_to_all(
            padded_den[slot_of_place].reshape(peer_count, per_owner, local_heads),
            "tok",
            split_axis=0,
            concat_axis=0,
            tiled=True,
        ),
    )
    back_num = got_num.reshape(buffer_rows, local_heads, LATENT)
    back_den = got_den.reshape(buffer_rows, local_heads)
    total_num = back_num[send_place] + self_weight[:, :, None] * new_entry[:, None, :LATENT].astype(
        jnp.float32
    )
    total_den = back_den[send_place] + self_weight
    mixed_latent = (total_num / total_den[:, :, None]).astype(jnp.bfloat16)
    head_out = jnp.einsum(
        "bhl,hld->bhd", mixed_latent, w_value_up, preferred_element_type=jnp.float32
    ).astype(jnp.bfloat16)
    head_out = head_out.reshape(local_rows, local_heads * NOPE)
    attn_piece = lax.psum_scatter(
        jnp.dot(head_out, w_out, preferred_element_type=jnp.float32),
        "head",
        scatter_dimension=1,
        tiled=True,
    )
    attended = (hidden.astype(jnp.float32) + attn_piece).astype(jnp.bfloat16)
    attended_wide = attended.astype(jnp.float32)
    gained = (attended_wide * ffn_gain).astype(jnp.bfloat16)
    squares, logit_part = lax.psum(
        (
            jnp.sum(attended_wide * attended_wide, axis=1),
            jnp.dot(gained, w_router, preferred_element_type=jnp.float32),
        ),
        "head",
    )
    inv_ffn = lax.rsqrt(squares / D + NORM_EPS)
    logits = logit_part * inv_ffn[:, None]
    normed_ffn = (attended_wide * ffn_gain * inv_ffn[:, None]).astype(jnp.bfloat16)
    expert_count = w_router.shape[1]
    route_count = routes.shape[1]
    expert_ids = jnp.arange(expert_count, dtype=jnp.int32)
    named = routes[:, :, None] == expert_ids[None, None, :]
    picked = jnp.sum(jnp.where(named, logits[:, None, :], 0.0), axis=2)
    lifted = jnp.exp(picked)
    route_weight = lifted / jnp.sum(lifted, axis=1, keepdims=True)
    struck = jnp.max(named.astype(jnp.int32), axis=1)
    earlier_hits = jnp.cumsum(struck, axis=0) - struck
    capacity = min(local_rows, max(2, 2 * local_rows * route_count // expert_count))
    route_place = routes * capacity + jnp.take_along_axis(earlier_hits, routes, axis=1)
    slot_total = expert_count * capacity
    slot_ids = jnp.arange(slot_total, dtype=jnp.int32)
    filled = route_place[None, :, :] == slot_ids[:, None, None]
    source_token = jnp.sum(
        jnp.where(filled, row_ids[None, :, None], 0), axis=(1, 2)
    ) + local_rows * (1 - jnp.max(filled.astype(jnp.int32), axis=(1, 2)))
    full_rows = lax.all_gather(normed_ffn, "head", axis=1, tiled=True)
    padded_rows = jnp.concatenate(
        [full_rows, jnp.zeros((1, full_rows.shape[1]), jnp.bfloat16)], axis=0
    )
    arrived = lax.all_to_all(
        padded_rows[source_token].reshape(expert_count, capacity, full_rows.shape[1]),
        "tok",
        split_axis=0,
        concat_axis=0,
        tiled=True,
    )
    expert_in = arrived.reshape(peer_count * capacity, full_rows.shape[1])
    gate_value = jnp.dot(expert_in, expert_gate[0], preferred_element_type=jnp.float32)
    up_value = jnp.dot(expert_in, expert_up[0], preferred_element_type=jnp.float32)
    activity = (jax.nn.silu(gate_value) * up_value).astype(jnp.bfloat16)
    expert_share = lax.psum_scatter(
        jnp.dot(activity, expert_down[0], preferred_element_type=jnp.float32).astype(jnp.bfloat16),
        "head",
        scatter_dimension=1,
        tiled=True,
    )
    returned = lax.all_to_all(
        expert_share.reshape(peer_count, capacity, quarter_width),
        "tok",
        split_axis=0,
        concat_axis=0,
        tiled=True,
    )
    chosen_rows = returned.reshape(slot_total, quarter_width)[route_place]
    expert_mix = jnp.sum(route_weight[:, :, None] * chosen_rows.astype(jnp.float32), axis=1).astype(
        jnp.bfloat16
    )
    return (new_entry, attended, expert_mix)


def solution(mesh):
    in_specs = (
        P("tok", "head"),
        P(),
        P(None, "head"),
        P("head", None),
        P("head", None, None),
        P("head", None, None),
        P("head", None),
        P(("tok", "head"), None),
        P("tok"),
        P("tok"),
        P("head"),
        P("head", None),
        P("tok", None),
        P("tok", None, "head"),
        P("tok", None, "head"),
        P("tok", "head", None),
    )
    out_specs = (P("tok", None), P("tok", "head"), P("tok", "head"))
    return jax.shard_map(body, mesh=mesh, in_specs=in_specs, out_specs=out_specs, check_vma=False)
```

profile of v0, /device:TPU:1, one launch (start us, length us, event | category | flops | bytes accessed | tf_op | source)
XLA Modules:
  0.0 640.7 jit_solution(2848119772154112607)
XLA Ops:
  7.2 10.6 %all_gather.18 = bf16[32,2048]{1,0:T(8,128)(2,1)S(1)} all-gather(bf16[32,512]{1,0:T(8,128)(2,1)} %param.16), channel_id=1, replica_groups=mesh['tok'=64,'head'=4] {'head'}, dimensions={1}, use_global_device_ids=true | all-gather | bytes 163840 | tf_op jit(solution)/shard_map/all_gather | solution.py:77
  23.0 46.7 %all-reduce.10.cloned.1.call-done = f32[32,576]{1,0:T(8,128)} async-done(((f32[32,576]{1,0:T(8,128)}), f32[32,576]{1,0:T(8,128)}) %all-reduce.10.cloned.1.call-update) | async-done | bytes 73744 | tf_op jit(solution)/shard_map/psum | solution.py:84
  74.0 246.6 %all-reduce.6 = (s32[2048]{0:T(1024)S(1)}, s32[2048]{0:T(1024)S(1)}) all-reduce(s32[2048]{0:T(1024)S(1)} %dynamic-update-slice.1, s32[2048]{0:T(1024)S(1)} %dynamic-update-slice), channel_id=1, replica_groups=mesh['tok'=64,'head'=4] {'tok'}, use_global_device_ids=true, to_apply=%add.4 | all-reduce | flops 4096 | bytes 32768
  324.8 14.7 %copy.84 = bf16[2048,4,576]{2,1,0:T(4,128)(2,1)} copy(bf16[2048,4,576]{2,0,1:T(8,128)(2,1)} %all-gather.3.cloned.1.call-done) | data formatting | bytes 18874368 | tf_op jit(solution)/shard_map/all_gather | solution.py:117
  339.5 4.7 gather_fusion.1
  344.3 10.5 %all-gather = bf16[32,16,576]{2,0,1:T(8,128)(2,1)S(1)} all-gather(bf16[32,4,576]{2,0,1:T(8,128)(2,1)S(1)} %copy.85), channel_id=2, replica_groups=mesh['tok'=64,'head'=4] {'head'}, dimensions={1}, use_global_device_ids=true | all-gather | bytes 737280 | tf_op jit(solution)/shard_map/all_gather | solution.py:133
  355.0 6.3 convert_reduce_fusion
  361.3 4.4 copy.87
  365.7 4.1 fusion
  374.4 13.0 %all-reduce.5 = f32[32,16]{1,0:T(8,128)S(1)} all-reduce(f32[32,16]{1,0:T(8,128)S(1)} %reduce_sum.110), channel_id=4, replica_groups=mesh['tok'=64,'head'=4] {'head'}, use_global_device_ids=true, to_apply=%region_11.12.clone | all-reduce | flops 512 | bytes 4096
  388.7 16.3 %all-to-all-start.1 = ((f32[64,1,4]{2,1,0:T(1,128)}), f32[64,1,4]{2,1,0:T(1,128)S(1)}, u32[]{:S(2)}, u32[]{:S(2)}) async-start(f32[64,1,4]{2,1,0:T(1,128)} %bitcast.18), calls=%async_computation.2 | async-start | bytes 65536 | tf_op jit(solution)/shard_map/all_to_all | solution.py:157
  414.4 7.3 %all-to-all-start = ((f32[64,1,4,512]{3,2,1,0:T(4,128)}), f32[64,1,4,512]{3,2,1,0:T(4,128)}, u32[]{:S(2)}, u32[]{:S(2)}) async-start(f32[64,1,4,512]{3,2,1,0:T(4,128)} %bitcast.72), calls=%async_computation.1 | async-start | bytes 1048576 | tf_op jit(solution)/shard_map/all_to_all | solution.py:150
  426.5 12.4 %all-to-all-done = f32[64,1,4,512]{3,2,1,0:T(4,128)} async-done(((f32[64,1,4,512]{3,2,1,0:T(4,128)}), f32[64,1,4,512]{3,2,1,0:T(4,128)}, u32[]{:S(2)}, u32[]{:S(2)}) %all-to-all-start) | async-done | bytes 524320 | tf_op jit(solution)/shard_map/all_to_all | solution.py:150
  447.0 14.9 %reduce-scatter.7.cloned.1.call-done = f32[32,512]{1,0:T(8,128)} async-done(((f32[32,2048]{1,0:T(8,128)}), f32[32,512]{1,0:T(8,128)}) %reduce-scatter.7.cloned.1.call-update) | async-done | bytes 65552 | tf_op jit(solution)/shard_map/reduce_scatter | solution.py:176
  463.1 11.8 %all-reduce.7 = (f32[32]{0:T(128)S(1)}, f32[32,64]{1,0:T(8,128)S(1)}) all-reduce(f32[32]{0:T(128)S(1)} %get-tuple-element.13, f32[32,64]{1,0:T(8,128)S(1)} %fusion.38), channel_id=1, replica_groups=mesh['tok'=64,'head'=4] {'head'}, use_global_device_ids=true, to_apply=%region_15.16 | all-reduce | flops 2080 | bytes 16640 | tf_op jit(solution)/shard_map/psum | solution.py:185
  474.9 9.3 %all_gather.23 = bf16[32,2048]{1,0:T(8,128)(2,1)S(1)} all-gather(bf16[32,512]{1,0:T(8,128)(2,1)S(1)} %fusion.36), channel_id=1, replica_groups=mesh['tok'=64,'head'=4] {'head'}, dimensions={1}, use_global_device_ids=true | all-gather | bytes 163840 | tf_op jit(solution)/shard_map/all_gather | solution.py:212
  487.4 3.7 reshape.358
  491.1 70.4 %all_to_all.20 = bf16[64,6,2048]{2,1,0:T(8,128)(2,1)} all-to-all(bf16[64,6,2048]{2,1,0:T(8,128)(2,1)} %reshape.358), channel_id=1, replica_groups=mesh['tok'=64,'head'=4] {'tok'}, dimensions={0} | all-to-all | bytes 3145728 | tf_op jit(solution)/shard_map/all_to_all | solution.py:216
  561.5 3.7 reshape.359
  565.3 3.6 fusion.8
  568.8 5.5 convolution_convert_fusion
  574.5 22.3 %reduce-scatter.9.cloned.1.call-done = bf16[384,512]{1,0:T(8,128)(2,1)} async-done(((bf16[384,2048]{1,0:T(8,128)(2,1)}), bf16[384,512]{1,0:T(8,128)(2,1)}) %reduce-scatter.9.cloned.1.call-update) | async-done | bytes 393232 | tf_op jit(solution)/shard_map/reduce_scatter | solution.py:227
  598.7 11.7 %all-to-all-start.3 = ((bf16[64,6,512]{2,1,0:T(8,128)(2,1)}), bf16[64,6,512]{2,1,0:T(8,128)(2,1)}, u32[]{:S(2)}, u32[]{:S(2)}) async-start(bf16[64,6,512]{2,1,0:T(8,128)(2,1)} %reshape.360), calls=%async_computation.6 | async-start | bytes 1048576 | tf_op jit(solution)/shard_map/all_to_all | solution.py:233
  612.1 15.5 %all-to-all-done.3 = bf16[64,6,512]{2,1,0:T(8,128)(2,1)} async-done(((bf16[64,6,512]{2,1,0:T(8,128)(2,1)}), bf16[64,6,512]{2,1,0:T(8,128)(2,1)}, u32[]{:S(2)}, u32[]{:S(2)}) %all-to-all-start.3) | async-done | bytes 393248 | tf_op jit(solution)/shard_map/all_to_all | solution.py:233
  (151 shorter events, 54.8 us)
Async XLA Ops:
  7.2 13.8 %copy-start = (bf16[2048,768]{1,0:T(8,128)(2,1)S(1)}, bf16[2048,768]{1,0:T(8,128)(2,1)}, u32[]{:S(2)}) copy-start(bf16[2048,768]{1,0:T(8,128)(2,1)} %param.18) | copy-start | bytes 9437188
  7.2 62.6 %all-reduce.10.cloned.1.call-start = ((), (), s32[]{:S(2)}) async-start(), calls=%async_computation.7 | async-start | bytes 163840 | tf_op jit(solution)/shard_map/psum | solution.py:84
  18.8 2.9 copy-start.14
  20.8 51.4 %copy-start.17 = (u32[256]{0:T(256)S(1)}, u32[256]{0:T(256)}, u32[]{:S(2)}) copy-start(u32[256]{0:T(256)} %constant.148) | copy-start | bytes 3076
  20.9 52.9 %copy-start.15 = (s32[32]{0:T(128)S(1)}, s32[32]{0:T(128)}, u32[]{:S(2)}) copy-start(s32[32]{0:T(128)} %param.25) | copy-start | bytes 388
  20.9 303.9 %all-gather.3.cloned.1.call-start = ((), (), s32[]{:S(2)}) async-start(), calls=%async_computation.8 | async-start | bytes 10649600 | tf_op jit(solution)/shard_map/all_gather | solution.py:117
  72.1 336.0 %reduce-scatter.5.cloned.1.call-start = ((), (), s32[]{:S(2)}) async-start(), calls=%async_computation.9 | async-start | bytes 1310720 | tf_op jit(solution)/shard_map/reduce_scatter | solution.py:138
  344.2 10.7 %copy-start.1 = (pred[512,2496]{0,1:T(32,128)(4,1)S(1)}, pred[512,2496]{0,1:T(32,128)(4,1)}, u32[]{:S(2)}) copy-start(pred[512,2496]{0,1:T(32,128)(4,1)} %copy.92) | copy-start | bytes 3833860
  369.8 2.8 copy-start.16
  374.0 31.8 %copy-start.13 = (s32[1024]{0:T(1024)}, s32[1024]{0:T(1024)S(1)}, u32[]{:S(2)}) copy-start(s32[1024]{0:T(1024)S(1)} %pad_clamp_fusion.3) | copy-start | bytes 12292
  388.7 25.7 %all-to-all-start.1 = ((f32[64,1,4]{2,1,0:T(1,128)}), f32[64,1,4]{2,1,0:T(1,128)S(1)}, u32[]{:S(2)}, u32[]{:S(2)}) async-start(f32[64,1,4]{2,1,0:T(1,128)} %bitcast.18), calls=%async_computation.2 | async-start | bytes 65536 | tf_op jit(solution)/shard_map/all_to_all | solution.py:157
  407.4 14.4 %copy-start.2 = (f32[32,576]{1,0:T(8,128)S(1)}, f32[32,576]{1,0:T(8,128)}, u32[]{:S(2)}) copy-start(f32[32,576]{1,0:T(8,128)} %all-reduce.10.cloned.1.call-done) | copy-start | bytes 221188
  414.4 24.5 %all-to-all-start = ((f32[64,1,4,512]{3,2,1,0:T(4,128)}), f32[64,1,4,512]{3,2,1,0:T(4,128)}, u32[]{:S(2)}, u32[]{:S(2)}) async-start(f32[64,1,4,512]{3,2,1,0:T(4,128)} %bitcast.72), calls=%async_computation.1 | async-start | bytes 1048576 | tf_op jit(solution)/shard_map/all_to_all | solution.py:150
  421.7 40.2 %reduce-scatter.7.cloned.1.call-start = ((), (), s32[]{:S(2)}) async-start(), calls=%async_computation.10 | async-start | bytes 327680 | tf_op jit(solution)/shard_map/reduce_scatter | solution.py:176
  440.8 21.1 %copy-start.6 = (bf16[32,512]{1,0:T(8,128)(2,1)S(1)}, bf16[32,512]{1,0:T(8,128)(2,1)}, u32[]{:S(2)}) copy-start(bf16[32,512]{1,0:T(8,128)(2,1)} %param.16) | copy-start | bytes 98308
  440.8 22.1 %copy-start.8 = (bf16[512,64]{0,1:T(8,128)(2,1)S(1)}, bf16[512,64]{0,1:T(8,128)(2,1)}, u32[]{:S(2)}) copy-start(bf16[512,64]{0,1:T(8,128)(2,1)} %param.27) | copy-start | bytes 196612
  440.8 22.1 %copy-start.11 = (f32[512]{0:T(512)S(1)}, f32[512]{0:T(512)}, u32[]{:S(2)}) copy-start(f32[512]{0:T(512)} %param.26) | copy-start | bytes 6148
  441.9 33.0 %copy-start.12 = (f32[512]{0:T(512)S(1)}, f32[512]{0:T(512)}, u32[]{:S(2)}) copy-start(f32[512]{0:T(512)} %param.26) | copy-start | bytes 6148
  445.9 150.9 %reduce-scatter.9.cloned.1.call-start = ((), (), s32[]{:S(2)}) async-start(), calls=%async_computation.11 | async-start | bytes 1966080 | tf_op jit(solution)/shard_map/reduce_scatter | solution.py:227
  462.9 12.0 %copy-start.3 = (bf16[32,512]{1,0:T(8,128)(2,1)}, bf16[32,512]{1,0:T(8,128)(2,1)S(1)}, u32[]{:S(2)}) copy-start(bf16[32,512]{1,0:T(8,128)(2,1)S(1)} %get-tuple-element.14) | copy-start | bytes 98308
  574.3 36.1 %copy-start.5 = (bf16[32,512]{1,0:T(8,128)(2,1)S(1)}, bf16[32,512]{1,0:T(8,128)(2,1)}, u32[]{:S(2)}) copy-start(bf16[32,512]{1,0:T(8,128)(2,1)} %copy-done.4) | copy-start | bytes 98308
  574.3 36.1 %copy-start.7 = (bf16[32,32]{1,0:T(8,128)(2,1)S(1)}, bf16[32,32]{1,0:T(8,128)(2,1)}, u32[]{:S(2)}) copy-start(bf16[32,32]{1,0:T(8,128)(2,1)} %get-tuple-element.26) | copy-start | bytes 6148
  574.3 36.9 %copy-start.10 = (s32[32,6]{0,1:T(8,128)S(1)}, s32[32,6]{0,1:T(8,128)}, u32[]{:S(2)}) copy-start(s32[32,6]{0,1:T(8,128)} %param.28) | copy-start | bytes 2308
  598.7 28.9 %all-to-all-start.3 = ((bf16[64,6,512]{2,1,0:T(8,128)(2,1)}), bf16[64,6,512]{2,1,0:T(8,128)(2,1)}, u32[]{:S(2)}, u32[]{:S(2)}) async-start(bf16[64,6,512]{2,1,0:T(8,128)(2,1)} %reshape.360), calls=%async_computation.6 | async-start | bytes 1048576 | tf_op jit(solution)/shard_map/all_to_all | solution.py:233
  (2 other events, 2.3 us)
Sparse Core Ops, SparseCore 0:
  21.0 48.7 all-reduce.9
  72.5 89.3 all-gather.2
  371.5 25.9 reduce-scatter.4
  446.1 15.8 reduce-scatter.6
  574.5 22.2 reduce-scatter.8
where the time goes:
time: 642 us; the launch traced here: 641 us
  blocking collectives  372 us (58%)
  waiting for transfers between devices  115 us (18%)
  local copies, waits for them, and re-layouts  60 us (9%)
  starting transfers between devices  35.5 us (6%)
  matrix products  28.6 us (4%)
  between operations  15.6 us (2%)
  other arithmetic  13.3 us (2%)
    unnamed x2, blocking collectives  260 us
    all_to_all x1, blocking collectives, body(): lax.all_to_all(padded_rows[source_token].reshape(expert_count, capacity,...  70.4 us
    psum x1, waiting for transfers between devices, body(): lax.psum(jnp.dot(normed_part, w_latent, preferred_element_type=jnp.float3...  46.7 us
    reduce_scatter x1, waiting for transfers between devices, body(): lax.psum_scatter(jnp.dot(activity, expert_down[0], preferred_element_type...  22.3 us
    all_to_all x1, starting transfers between devices, body(): lax.all_to_all(padded_den[slot_of_place].reshape(peer_count, per_owner, l...  16.3 us
    all_to_all x1, waiting for transfers between devices, body(): lax.all_to_all(expert_share.reshape(peer_count, capacity, quarter_width),...  15.5 us
    reduce_scatter x1, waiting for transfers between devices, body(): lax.psum_scatter(jnp.dot(head_out, w_out, preferred_element_type=jnp.floa...  14.9 us
    all_gather x1, local copies, waits for them, and re-layouts, body(): lax.all_gather(probes, 'tok', axis=0, tiled=True)  14.7 us
  transfers between devices with their start and end apart: 8, of which 6 were waited for; matrix products, arithmetic and copies ran while one was open for 4% of the time, Pallas kernels for 0%

commit v1 on v0

--- a/solution.py
+++ b/solution.py
@@ -8,6 +8,11 @@
 ROPE = 64
 LATENT = 512
 NORM_EPS = 1e-06
+
+
+def _number_pages(local_x):
+    moved = jnp.sum(lax.all_gather(local_x, "head"), 0)
+    return moved
 
 
 def rotate_pairs(values, places):
@@ -81,9 +86,7 @@
     normed_part = lax.dynamic_slice_in_dim(
         normed_attn, head_index * quarter_width, quarter_width, 1
     )
-    compressed = lax.psum(
-        jnp.dot(normed_part, w_latent, preferred_element_type=jnp.float32), "head"
-    )
+    compressed = _number_pages(jnp.dot(normed_part, w_latent, preferred_element_type=jnp.float32))
     latent_new = compressed[:, :LATENT]
     latent_new = latent_new * lax.rsqrt(
         jnp.mean(latent_new * latent_new, axis=1, keepdims=True) + NORM_EPS

time: 642 us -> 615 us (0.958)
  waiting for transfers between devices: 115 us -> 70.9 us
  blocking collectives: 372 us -> 387 us
    psum x1 -> x0, waiting for transfers between devices: 46.7 us -> none  [body(): lax.psum(jnp.dot(normed_part, w_latent, preferred_element_type=jnp.float3...]
    all_gather x0 -> x1, blocking collectives: none -> 9.51 us  [_number_pages(): moved = jnp.sum(lax.all_gather(local_x, 'head'), 0)]
  transfers between devices with their start and end apart: 8 -> 7, of which waited for: 6 -> 5; matrix products, arithmetic and copies ran while one was open for 4% -> 4% of each run, Pallas kernels for 0% -> 0%
where the time goes in v1:
time: 615 us; the launch traced here: 613 us
  blocking collectives  387 us (63%)
  waiting for transfers between devices  70.9 us (12%)
  local copies, waits for them, and re-layouts  63.2 us (10%)
  starting transfers between devices  32.7 us (5%)
  matrix products  27.8 us (5%)
  other arithmetic  16.2 us (3%)
  between operations  15.7 us (3%)
    unnamed x2, blocking collectives  265 us
    all_to_all x1, blocking collectives, body(): lax.all_to_all(padded_rows[source_token].reshape(expert_count, capacity,...  70.4 us
    reduce_scatter x1, waiting for transfers between devices, body(): lax.psum_scatter(jnp.dot(activity, expert_down[0], preferred_element_type...  21.6 us
    all_to_all x1, waiting for transfers between devices, body(): lax.all_to_all(expert_share.reshape(peer_count, capacity, quarter_width),...  16.2 us
    all_to_all x1, starting transfers between devices, body(): lax.all_to_all(padded_den[slot_of_place].reshape(peer_count, per_owner, l...  15.3 us
    reduce_scatter x1, waiting for transfers between devices, body(): lax.psum_scatter(jnp.dot(head_out, w_out, preferred_element_type=jnp.floa...  15 us
    all_gather x1, local copies, waits for them, and re-layouts, body(): lax.all_gather(probes, 'tok', axis=0, tiled=True)  14.8 us
  transfers between devices with their start and end apart: 7, of which 5 were waited for; matrix products, arithmetic and copies ran while one was open for 4% of the time, Pallas kernels for 0%

profile of v1, /device:TPU:1, one launch (start us, length us, event | category | flops | bytes accessed | tf_op | source)
XLA Modules:
  0.0 613.4 jit_solution(11631702008648657482)
XLA Ops:
  7.8 10.6 %all_gather.24 = bf16[32,2048]{1,0:T(8,128)(2,1)S(1)} all-gather(bf16[32,512]{1,0:T(8,128)(2,1)} %param.16), channel_id=1, replica_groups=mesh['tok'=64,'head'=4] {'head'}, dimensions={1}, use_global_device_ids=true | all-gather | bytes 163840 | tf_op jit(solution)/shard_map/all_gather | solution.py:82
  22.1 9.5 %all-gather = f32[128,576]{1,0:T(8,128)S(1)} all-gather(f32[32,576]{1,0:T(8,128)S(1)} %fusion.45), channel_id=2, replica_groups=mesh['tok'=64,'head'=4] {'head'}, dimensions={0}, use_global_device_ids=true | all-gather | bytes 368640 | tf_op jit(solution)/shard_map/all_gather | solution.py:14
  41.0 251.0 %all-reduce.6 = (s32[2048]{0:T(1024)S(1)}, s32[2048]{0:T(1024)S(1)}) all-reduce(s32[2048]{0:T(1024)S(1)} %dynamic-update-slice.1, s32[2048]{0:T(1024)S(1)} %dynamic-update-slice), channel_id=1, replica_groups=mesh['tok'=64,'head'=4] {'tok'}, use_global_device_ids=true, to_apply=%add.4 | all-reduce | flops 4096 | bytes 32768
  296.8 14.8 %copy.84 = bf16[2048,4,576]{2,1,0:T(4,128)(2,1)} copy(bf16[2048,4,576]{2,0,1:T(8,128)(2,1)} %all-gather.4.cloned.1.call-done) | data formatting | bytes 18874368 | tf_op jit(solution)/shard_map/all_gather | solution.py:120
  311.6 4.7 gather_fusion.1
  316.3 10.5 %all-gather.1 = bf16[32,16,576]{2,0,1:T(8,128)(2,1)S(1)} all-gather(bf16[32,4,576]{2,0,1:T(8,128)(2,1)S(1)} %copy.85), channel_id=3, replica_groups=mesh['tok'=64,'head'=4] {'head'}, dimensions={1}, use_global_device_ids=true | all-gather | bytes 737280 | tf_op jit(solution)/shard_map/all_gather | solution.py:136
  327.0 6.3 %convert_reduce_fusion = (f32[512]{0:T(512)S(1)}, bf16[512,2496]{0,1:T(8,128)(2,1)}) fusion(pred[512,2496]{0,1:T(32,128)(4,1)S(1)} %copy-done.1, bf16[512,576]{1,0:T(8,128)(2,1)S(1)} %bitcast.76, bf16[2496,576]{0,1:T(8,128)(2,1)} %param.23), kind=kOutput, calls=%fused_computation.11 | convolution fusion | flops 1478589952 | bytes 7301120 | tf_op jit(solution)/shard_map/qc,pc->qp/dot_general | solution.py:42
  333.3 4.4 copy.87
  337.7 4.1 fusion
  348.3 13.9 %all-reduce.5 = f32[32,16]{1,0:T(8,128)S(1)} all-reduce(f32[32,16]{1,0:T(8,128)S(1)} %reduce_sum.120), channel_id=5, replica_groups=mesh['tok'=64,'head'=4] {'head'}, use_global_device_ids=true, to_apply=%region_11.12.clone | all-reduce | flops 512 | bytes 4096
  363.5 15.3 %all-to-all-start.1 = ((f32[64,1,4]{2,1,0:T(1,128)}), f32[64,1,4]{2,1,0:T(1,128)S(1)}, u32[]{:S(2)}, u32[]{:S(2)}) async-start(f32[64,1,4]{2,1,0:T(1,128)} %bitcast.19), calls=%async_computation.2 | async-start | bytes 65536 | tf_op jit(solution)/shard_map/all_to_all | solution.py:160
  381.8 6.4 %all-to-all-done.1 = f32[64,1,4]{2,1,0:T(1,128)S(1)} async-done(((f32[64,1,4]{2,1,0:T(1,128)}), f32[64,1,4]{2,1,0:T(1,128)S(1)}, u32[]{:S(2)}, u32[]{:S(2)}) %all-to-all-start.1) | async-done | bytes 1056 | tf_op jit(solution)/shard_map/all_to_all | solution.py:160
  388.2 5.5 all-to-all-start
  399.3 11.6 %all-to-all-done = f32[64,1,4,512]{3,2,1,0:T(4,128)} async-done(((f32[64,1,4,512]{3,2,1,0:T(4,128)}), f32[64,1,4,512]{3,2,1,0:T(4,128)}, u32[]{:S(2)}, u32[]{:S(2)}) %all-to-all-start) | async-done | bytes 524320 | tf_op jit(solution)/shard_map/all_to_all | solution.py:153
  419.0 15.0 %reduce-scatter.7.cloned.1.call-done = f32[32,512]{1,0:T(8,128)} async-done(((f32[32,2048]{1,0:T(8,128)}), f32[32,512]{1,0:T(8,128)}) %reduce-scatter.7.cloned.1.call-update) | async-done | bytes 65552 | tf_op jit(solution)/shard_map/reduce_scatter | solution.py:179
  435.8 11.8 %all-reduce.7 = (f32[32]{0:T(128)S(1)}, f32[32,64]{1,0:T(8,128)S(1)}) all-reduce(f32[32]{0:T(128)S(1)} %get-tuple-element.13, f32[32,64]{1,0:T(8,128)S(1)} %fusion.38), channel_id=1, replica_groups=mesh['tok'=64,'head'=4] {'head'}, use_global_device_ids=true, to_apply=%region_15.16 | all-reduce | flops 2080 | bytes 16640 | tf_op jit(solution)/shard_map/psum | solution.py:188
  447.7 9.3 %all_gather.31 = bf16[32,2048]{1,0:T(8,128)(2,1)S(1)} all-gather(bf16[32,512]{1,0:T(8,128)(2,1)S(1)} %fusion.36), channel_id=1, replica_groups=mesh['tok'=64,'head'=4] {'head'}, dimensions={1}, use_global_device_ids=true | all-gather | bytes 163840 | tf_op jit(solution)/shard_map/all_gather | solution.py:215
  460.1 3.7 reshape.358
  463.9 70.4 %all_to_all.20 = bf16[64,6,2048]{2,1,0:T(8,128)(2,1)} all-to-all(bf16[64,6,2048]{2,1,0:T(8,128)(2,1)} %reshape.358), channel_id=1, replica_groups=mesh['tok'=64,'head'=4] {'tok'}, dimensions={0} | all-to-all | bytes 3145728 | tf_op jit(solution)/shard_map/all_to_all | solution.py:219
  534.3 3.7 reshape.359
  541.6 5.5 convolution_convert_fusion
  547.9 21.6 %reduce-scatter.9.cloned.1.call-done = bf16[384,512]{1,0:T(8,128)(2,1)} async-done(((bf16[384,2048]{1,0:T(8,128)(2,1)}), bf16[384,512]{1,0:T(8,128)(2,1)}) %reduce-scatter.9.cloned.1.call-update) | async-done | bytes 393232 | tf_op jit(solution)/shard_map/reduce_scatter | solution.py:230
  571.4 11.7 %all-to-all-start.3 = ((bf16[64,6,512]{2,1,0:T(8,128)(2,1)}), bf16[64,6,512]{2,1,0:T(8,128)(2,1)}, u32[]{:S(2)}, u32[]{:S(2)}) async-start(bf16[64,6,512]{2,1,0:T(8,128)(2,1)} %reshape.360), calls=%async_computation.6 | async-start | bytes 1048576 | tf_op jit(solution)/shard_map/all_to_all | solution.py:236
  584.2 16.2 %all-to-all-done.3 = bf16[64,6,512]{2,1,0:T(8,128)(2,1)} async-done(((bf16[64,6,512]{2,1,0:T(8,128)(2,1)}), bf16[64,6,512]{2,1,0:T(8,128)(2,1)}, u32[]{:S(2)}, u32[]{:S(2)}) %all-to-all-start.3) | async-done | bytes 393248 | tf_op jit(solution)/shard_map/all_to_all | solution.py:236
  (170 shorter events, 60.1 us)
Async XLA Ops:
  7.2 12.2 %copy-start = (bf16[2048,768]{1,0:T(8,128)(2,1)S(1)}, bf16[2048,768]{1,0:T(8,128)(2,1)}, u32[]{:S(2)}) copy-start(bf16[2048,768]{1,0:T(8,128)(2,1)} %param.18) | copy-start | bytes 9437188
  7.2 289.6 %all-gather.4.cloned.1.call-start = ((), (), s32[]{:S(2)}) async-start(), calls=%async_computation.7 | async-start | bytes 10649600 | tf_op jit(solution)/shard_map/all_gather | solution.py:120
  19.3 12.3 %copy-start.25 = (s32[32]{0:T(128)S(1)}, s32[32]{0:T(128)}, u32[]{:S(2)}) copy-start(s32[32]{0:T(128)} %param.24) | copy-start | bytes 388
  37.3 341.7 %reduce-scatter.5.cloned.1.call-start = ((), (), s32[]{:S(2)}) async-start(), calls=%async_computation.8 | async-start | bytes 1310720 | tf_op jit(solution)/shard_map/reduce_scatter | solution.py:141
  292.0 4.8 copy-start.11
  292.2 19.3 %copy-start.19 = (s32[1024]{0:T(1024)}, s32[1024]{0:T(1024)S(1)}, u32[]{:S(2)}) copy-start(s32[1024]{0:T(1024)S(1)} %pad_clamp_fusion.4) | copy-start | bytes 12292
  316.3 10.7 %copy-start.1 = (pred[512,2496]{0,1:T(32,128)(4,1)S(1)}, pred[512,2496]{0,1:T(32,128)(4,1)}, u32[]{:S(2)}) copy-start(pred[512,2496]{0,1:T(32,128)(4,1)} %copy.92) | copy-start | bytes 3833860
  333.3 4.4 copy-start.4
  344.8 17.4 %copy-start.8 = (s32[32,6]{1,0:T(8,128)}, s32[32,6]{1,0:T(8,128)S(1)}, u32[]{:S(2)}) copy-start(s32[32,6]{1,0:T(8,128)S(1)} %copy.97) | copy-start | bytes 2308
  363.5 24.7 %all-to-all-start.1 = ((f32[64,1,4]{2,1,0:T(1,128)}), f32[64,1,4]{2,1,0:T(1,128)S(1)}, u32[]{:S(2)}, u32[]{:S(2)}) async-start(f32[64,1,4]{2,1,0:T(1,128)} %bitcast.19), calls=%async_computation.2 | async-start | bytes 65536 | tf_op jit(solution)/shard_map/all_to_all | solution.py:160
  378.9 14.8 %copy-start.24 = (s32[32]{0:T(128)S(1)}, s32[32]{0:T(128)}, u32[]{:S(2)}) copy-start(s32[32]{0:T(128)} %compare_select_fusion.3) | copy-start | bytes 388
  388.2 22.8 %all-to-all-start = ((f32[64,1,4,512]{3,2,1,0:T(4,128)}), f32[64,1,4,512]{3,2,1,0:T(4,128)}, u32[]{:S(2)}, u32[]{:S(2)}) async-start(f32[64,1,4,512]{3,2,1,0:T(4,128)} %bitcast.73), calls=%async_computation.1 | async-start | bytes 1048576 | tf_op jit(solution)/shard_map/all_to_all | solution.py:153
  393.7 40.3 %reduce-scatter.7.cloned.1.call-start = ((), (), s32[]{:S(2)}) async-start(), calls=%async_computation.9 | async-start | bytes 327680 | tf_op jit(solution)/shard_map/reduce_scatter | solution.py:179
  393.7 4.4 copy-start.20
  397.7 13.2 %copy-start.6 = (bf16[32,512]{1,0:T(8,128)(2,1)}, bf16[32,512]{1,0:T(8,128)(2,1)S(1)}, u32[]{:S(2)}) copy-start(bf16[32,512]{1,0:T(8,128)(2,1)S(1)} %get-tuple-element.16) | copy-start | bytes 98308
  410.9 7.1 %copy-start.9 = (s32[32,6]{1,0:T(8,128)S(1)}, s32[32,6]{1,0:T(8,128)}, u32[]{:S(2)}) copy-start(s32[32,6]{1,0:T(8,128)} %copy-done.8) | copy-start | bytes 2308
  412.8 21.2 %copy-start.10 = (bf16[32,512]{1,0:T(8,128)(2,1)S(1)}, bf16[32,512]{1,0:T(8,128)(2,1)}, u32[]{:S(2)}) copy-start(bf16[32,512]{1,0:T(8,128)(2,1)} %param.16) | copy-start | bytes 98308
  412.8 22.1 %copy-start.15 = (bf16[512,64]{0,1:T(8,128)(2,1)S(1)}, bf16[512,64]{0,1:T(8,128)(2,1)}, u32[]{:S(2)}) copy-start(bf16[512,64]{0,1:T(8,128)(2,1)} %param.27) | copy-start | bytes 196612
  413.9 33.7 %copy-start.18 = (f32[512]{0:T(512)S(1)}, f32[512]{0:T(512)}, u32[]{:S(2)}) copy-start(f32[512]{0:T(512)} %param.26) | copy-start | bytes 6148
  417.9 151.6 %reduce-scatter.9.cloned.1.call-start = ((), (), s32[]{:S(2)}) async-start(), calls=%async_computation.10 | async-start | bytes 1966080 | tf_op jit(solution)/shard_map/reduce_scatter | solution.py:230
  435.0 12.7 %copy-start.5 = (bf16[32,512]{1,0:T(8,128)(2,1)}, bf16[32,512]{1,0:T(8,128)(2,1)S(1)}, u32[]{:S(2)}) copy-start(bf16[32,512]{1,0:T(8,128)(2,1)S(1)} %get-tuple-element.14) | copy-start | bytes 98308
  541.6 5.6 copy-start.7
  547.1 36.2 %copy-start.17 = (s32[32,6]{0,1:T(8,128)S(1)}, s32[32,6]{0,1:T(8,128)}, u32[]{:S(2)}) copy-start(s32[32,6]{0,1:T(8,128)} %param.28) | copy-start | bytes 2308
  571.4 28.9 %all-to-all-start.3 = ((bf16[64,6,512]{2,1,0:T(8,128)(2,1)}), bf16[64,6,512]{2,1,0:T(8,128)(2,1)}, u32[]{:S(2)}, u32[]{:S(2)}) async-start(bf16[64,6,512]{2,1,0:T(8,128)(2,1)} %reshape.360), calls=%async_computation.6 | async-start | bytes 1048576 | tf_op jit(solution)/shard_map/all_to_all | solution.py:236
  (11 other events, 29.1 us)
Sparse Core Ops, SparseCore 0:
  37.4 94.7 all-gather.3
  343.6 25.8 reduce-scatter.4
  418.1 15.8 reduce-scatter.6
  547.2 22.2 reduce-scatter.8
